TPU v7x, 512 devices: a whole 4x8x8 slice. The times are simulated.
512 devices in a mesh: ctx: 128 (over y, z, core), tp: 4 (over x).
Axes of the slice: x: 4, y: 8, z: 8, core: 2. Of those that a mesh axis runs over, the one named last changes fastest.
Arguments:
- hidden_in: bfloat16 [16384, 1536], P('ctx', 'tp'), may hold values from -60 to 60
- queries: bfloat16 [16384, 2048], P('ctx', 'tp'), may hold values from -200 to 200
- rotated_key_value: bfloat16 [16384, 4, 128], P('ctx', 'tp'), may hold values from -5 to 5
- sink_logit_table: float32 [32], P('tp'), may hold values from -2 to 2
- out_proj: bfloat16 [2048, 1536], P('tp', 'ctx'), may hold values from -0.125 to 0.125
- norm_gain: float32 [1536], P('tp'), may hold values from 0.1 to 1.9
- expert_in: bfloat16 [128, 2, 1536, 1536], P('ctx', None, None, 'tp'), may hold values from -0.15625 to 0.15625
- expert_out: bfloat16 [128, 1536, 1536], P('ctx', 'tp'), may hold values from -0.15625 to 0.15625
- routes: int32 [16384, 4], P('ctx'), may hold values from 0 to 127, all different within a row; in each aligned block of 128 rows (0 to 127, 128 to 255, ...) at most 12 rows name the same one
- route_scores: float32 [16384, 4], P('ctx'), may hold values from 0.05 to 1
Outputs:
- layer_out: bfloat16 [16384, 1536], P('ctx', 'tp')
Inputs may be any that keep to these rules, and one draw needn't show every extreme that they name: `routes`: each token names 4 different experts. In every aligned block of 128 tokens (the tokens of one device) no expert is named by more than 12 tokens, a bound that some block reaches.
All inputs are finite; a program needn't handle non-finite values.
Results may differ from a plain program's by a relative error of at most 0.008.
Values may be sent and summed in bfloat16 or wider, within the bound.
No kernel may reach another device: no remote copies, remote signals or barrier semaphores. Data moves between devices by JAX's collectives and lax.ppermute only.
A program may use at most 64 MiB of HBM per device.

v0:
```python
import jax
import jax.numpy as jnp
from jax import lax
from jax.sharding import PartitionSpec as P

WINDOW_KEYS = 128


def shifted(value, axis, steps):
    count = lax.axis_size(axis)
    first, last = (max(0, -steps), min(count, count - steps))
    return lax.ppermute(value, axis, [(source, source + steps) for source in range(first, last)])


def attend(query_block, key_blk, value_blk, inside, sink_row_block, factor):
    score = (
        jnp.einsum("rgqd,sgd->gqrs", query_block, key_blk, preferred_element_type=jnp.float32)
        * factor
    )
    masked = jnp.where(inside, score, -1e30)
    top_score = jnp.maximum(jnp.max(masked, -1), sink_row_block[:, :, None])
    expvals = jnp.where(inside, jnp.exp(score - top_score[..., None]), 0.0)
    denominator = jnp.sum(expvals, -1) + jnp.exp(sink_row_block[:, :, None] - top_score)
    probs = (expvals / denominator[..., None]).astype(jnp.bfloat16)
    mixed = jnp.einsum("gqrs,sgd->rgqd", probs, value_blk, preferred_element_type=jnp.float32)
    return mixed.astype(jnp.bfloat16)


def body(
    hidden_in,
    queries,
    rotated_key_value,
    sink_logit_table,
    out_proj,
    norm_gain,
    expert_in,
    expert_out,
    routes,
    route_scores,
):
    tok_rows = hidden_in.shape[0]
    kv_heads = rotated_key_value.shape[1]
    head_dim = rotated_key_value.shape[2] // 2
    q_heads = sink_logit_table.shape[0]
    queries_per_group = q_heads // kv_heads
    factor = head_dim ** (-0.5)
    sink_row_block = sink_logit_table.reshape(kv_heads, queries_per_group)
    earlier = shifted(rotated_key_value, "ctx", 1)
    keys_all = jnp.concatenate([earlier, rotated_key_value], 0)
    first_pos = lax.axis_index("ctx") * tok_rows
    block_row_count = min(512, tok_rows)
    query_block = queries.reshape(block_row_count, kv_heads, queries_per_group, head_dim)
    query_pos = first_pos + 0 + jnp.arange(block_row_count, dtype=jnp.int32)[:, None]
    key_pos = (
        first_pos
        + 0
        - WINDOW_KEYS
        + jnp.arange(block_row_count + WINDOW_KEYS, dtype=jnp.int32)[None, :]
    )
    inside = (key_pos <= query_pos) & (key_pos > query_pos - WINDOW_KEYS) & (key_pos >= 0)
    mixed = attend(
        query_block,
        keys_all[..., :head_dim],
        keys_all[..., head_dim:],
        inside,
        sink_row_block,
        factor,
    )
    outputs = mixed.reshape(block_row_count, q_heads * head_dim)
    head_partial = jnp.dot(
        outputs,
        lax.all_gather(out_proj, "ctx", axis=1, tiled=True),
        preferred_element_type=jnp.float32,
    )
    d_model = head_partial.shape[1]
    residual = hidden_in.astype(jnp.float32) + lax.psum_scatter(
        head_partial.astype(jnp.bfloat16), "tp", scatter_dimension=1, tiled=True
    ).astype(jnp.float32)
    square_total = lax.psum(jnp.sum(residual * residual, -1), "tp")
    normed = (residual * lax.rsqrt(square_total[:, None] / d_model + 1e-05) * norm_gain).astype(
        jnp.bfloat16
    )
    ctx_count = lax.axis_size("ctx")
    tp_count = lax.axis_size("tp")
    top_count = routes.shape[1]
    experts = ctx_count * expert_in.shape[0]
    capacity = max(2, min(tok_rows, 3 * top_count * tok_rows // experts))
    quarter_w = d_model // tp_count
    onehot = (routes[:, :, None] == jnp.arange(experts, dtype=jnp.int32)).astype(jnp.int32)
    per_tok = jnp.sum(onehot, 1)
    before = jnp.cumsum(per_tok, axis=0) - per_tok
    slot_ids = jnp.sum(onehot * before[:, None, :], -1)
    flat_index = (routes * capacity + slot_ids).reshape(-1)
    weights = route_scores / jnp.sum(route_scores, -1, keepdims=True)
    full_data = lax.all_gather(normed, "tp", axis=1, tiled=True)
    row_width = full_data.shape[1]
    spread = jnp.broadcast_to(full_data[:, None, :], (tok_rows, top_count, row_width)).reshape(
        -1, row_width
    )
    outbox = jnp.zeros((experts * capacity, row_width), jnp.bfloat16).at[flat_index].set(spread)
    arrived = lax.all_to_all(
        outbox.reshape(ctx_count, 1, capacity, row_width),
        "ctx",
        split_axis=0,
        concat_axis=1,
        tiled=True,
    )
    leading = arrived.shape[:3]
    row_data = arrived.reshape(-1, d_model)
    gate_vals = jnp.dot(row_data, expert_in[0, 0], preferred_element_type=jnp.float32)
    up_vals = jnp.dot(row_data, expert_in[0, 1], preferred_element_type=jnp.float32)
    activated = ((up_vals + 1.0) * gate_vals * jax.nn.sigmoid(1.702 * gate_vals)).astype(
        jnp.bfloat16
    )
    partial_value = jnp.dot(activated, expert_out[0], preferred_element_type=jnp.float32).astype(
        jnp.bfloat16
    )
    result = partial_value.reshape(leading + (d_model,))
    returned = lax.all_to_all(result, "ctx", split_axis=1, concat_axis=0, tiled=True)
    picked = returned.reshape(-1, d_model)[flat_index].reshape(tok_rows, top_count, d_model)
    expert_result = lax.psum_scatter(
        picked.astype(jnp.float32).astype(jnp.bfloat16), "tp", scatter_dimension=2, tiled=True
    )
    moe_sum = jnp.zeros((tok_rows, quarter_w), jnp.float32)
    for member in range(top_count):
        moe_sum = moe_sum + weights[:, member : member + 1] * expert_result[:, member].astype(
            jnp.float32
        )
    return (residual + moe_sum).astype(jnp.bfloat16)


def solution(mesh):
    in_specs = (
        P("ctx", "tp"),
        P("ctx", "tp"),
        P("ctx", "tp", None),
        P("tp"),
        P("tp", "ctx"),
        P("tp"),
        P("ctx", None, None, "tp"),
        P("ctx", "tp", None),
        P("ctx", None),
        P("ctx", None),
    )
    out_specs = P("ctx", "tp")
    return jax.shard_map(body, mesh=mesh, in_specs=in_specs, out_specs=out_specs, check_vma=False)
```

profile of v0, /device:TPU:1, one launch (start us, length us, event | category | flops | bytes accessed | tf_op | source)
XLA Modules:
  0.0 596.0 jit_solution(12314358451730001000)
XLA Ops:
  8.2 5.4 collective-permute-start
  14.8 2.2 collective-permute-done
  18.7 80.7 %all-gather.3.cloned.1.call-done = bf16[128,12,512]{2,1,0:T(8,128)(2,1)} async-done(((bf16[1,12,512]{2,1,0:T(8,128)(2,1)}), bf16[128,12,512]{2,1,0:T(8,128)(2,1)}) %all-gather.3.cloned.1.call-update) | async-done | bytes 1572880 | tf_op jit(solution)/shard_map/all_gather | solution.py:72
  99.4 2.5 reshape.218
  104.4 19.8 %reduce-scatter.7.cloned.1.call-done = bf16[384,128]{1,0:T(8,128)(2,1)} async-done(((bf16[1536,128]{1,0:T(8,128)(2,1)}), bf16[384,128]{1,0:T(8,128)(2,1)}) %reduce-scatter.7.cloned.1.call-update) | async-done | bytes 98320
  125.4 6.9 %psum.7 = f32[128]{0:T(128)S(1)} all-reduce(f32[128]{0:T(128)S(1)} %multiply_reduce_fusion), channel_id=1, replica_groups=mesh['ctx'=128,'tp'=4] {'tp'}, use_global_device_ids=true, to_apply=%region_8.9 | all-reduce | flops 128 | bytes 1024 | tf_op jit(solution)/shard_map/psum | solution.py:79
  132.4 10.0 %all_gather.7 = bf16[128,1536]{1,0:T(8,128)(2,1)S(1)} all-gather(bf16[128,384]{1,0:T(8,128)(2,1)S(1)} %multiply_convert_fusion), channel_id=1, replica_groups=mesh['ctx'=128,'tp'=4] {'tp'}, dimensions={1}, use_global_device_ids=true | all-gather | bytes 491520 | tf_op jit(solution)/shard_map/all_gather | solution.py:95
  142.8 1.4 reshape.213
  144.2 6.9 %scatter_custom_fusion = bf16[1536,1536]{1,0:T(8,128)(2,1)} fusion(s32[512]{0:T(512)S(1)} %bitcast.86, bf16[512,1536]{1,0:T(8,128)(2,1)} %reshape.213, bf16[]{:T(256)} %constant.14.clone.1), kind=kCustom, calls=%fused_computation.8 | custom fusion | bytes 4719104 | tf_op jit(solution)/shard_map/scatter | solution.py:100
  151.0 8.1 %reshape.192 = bf16[128,1,12,1536]{3,2,0,1:T(8,128)(2,1)} reshape(bf16[1536,1536]{1,0:T(8,128)(2,1)} %scatter_custom_fusion) | data formatting | bytes 9437184 | tf_op jit(solution)/shard_map/reshape | solution.py:102
  159.1 164.5 %all_to_all.8 = bf16[128,1,12,1536]{3,2,1,0:T(8,128)(2,1)} all-to-all(bf16[128,1,12,1536]{3,2,1,0:T(8,128)(2,1)} %bitcast.77), channel_id=1, replica_groups=mesh['ctx'=128,'tp'=4] {'ctx'}, dimensions={0} | all-to-all | bytes 9437184 | tf_op jit(solution)/shard_map/all_to_all | solution.py:101
  323.6 8.2 %reshape.193 = bf16[1536,1536]{1,0:T(8,128)(2,1)} reshape(bf16[128,1,12,1536]{3,2,1,0:T(8,128)(2,1)} %all_to_all.8) | data formatting | bytes 9437184 | tf_op jit(solution)/shard_map/reshape | solution.py:109
  331.8 6.7 %fusion.7 = f32[1536,384]{1,0:T(8,128)} fusion(bf16[1536,1536]{1,0:T(8,128)(2,1)} %reshape.193, bf16[1,2,1536,384]{3,2,1,0:T(8,128)(2,1)} %param.16), kind=kOutput, calls=%fused_computation.14 | convolution fusion | flops 1811939328 | bytes 8257536 | tf_op jit(solution)/shard_map/dot_general | solution.py:110
  338.5 9.1 %convolution_convert_fusion = bf16[1536,1536]{1,0:T(8,128)(2,1)} fusion(bf16[1,384,1536]{2,1,0:T(8,128)(2,1)S(1)} %copy-done, f32[1536,384]{1,0:T(8,128)} %fusion.7, bf16[1536,1536]{1,0:T(8,128)(2,1)} %reshape.193, bf16[1,2,1536,384]{3,2,1,0:T(8,128)(2,1)} %param.16), kind=kOutput, calls=%fused_computation.2 | convolution fusion | flops 3630956544 | bytes 14155776 | tf_op jit(solution)/shard_map/dot_general | solution.py:115
  347.6 8.1 %reshape.194 = bf16[1,128,12,1536]{3,2,1,0:T(8,128)(2,1)} reshape(bf16[1536,1536]{1,0:T(8,128)(2,1)} %convolution_convert_fusion) | data formatting | bytes 9437184 | tf_op jit(solution)/shard_map/reshape | solution.py:118
  355.6 17.5 %all-to-all-start.1 = ((bf16[1,128,12,1536]{3,2,0,1:T(8,128)(2,1)}), bf16[1,128,12,1536]{3,2,0,1:T(8,128)(2,1)}, u32[]{:S(2)}, u32[]{:S(2)}) async-start(bf16[1,128,12,1536]{3,2,0,1:T(8,128)(2,1)} %bitcast.76), calls=%async_computation.1 | async-start | bytes 12582912 | tf_op jit(solution)/shard_map/all_to_all | solution.py:119
  373.3 153.9 %all-to-all-done.1 = bf16[1,128,12,1536]{3,2,0,1:T(8,128)(2,1)} async-done(((bf16[1,128,12,1536]{3,2,0,1:T(8,128)(2,1)}), bf16[1,128,12,1536]{3,2,0,1:T(8,128)(2,1)}, u32[]{:S(2)}, u32[]{:S(2)}) %all-to-all-start.1) | async-done | bytes 4718624 | tf_op jit(solution)/shard_map/all_to_all | solution.py:119
  527.2 8.2 %reshape.195 = bf16[1536,1536]{1,0:T(8,128)(2,1)} reshape(bf16[1,128,12,1536]{3,2,0,1:T(8,128)(2,1)} %all-to-all-done.1) | data formatting | bytes 9437184 | tf_op jit(solution)/shard_map/reshape | solution.py:120
  535.4 7.4 %gather_fusion = bf16[512,1536]{1,0:T(8,128)(2,1)} fusion(bf16[1536,1536]{1,0:T(8,128)(2,1)} %reshape.195, s32[1024]{0:T(1024)S(1)} %pad_clamp_fusion), kind=kCustom, calls=%fused_computation | custom fusion | bytes 3147776 | tf_op jit(solution)/shard_map/gather | solution.py:120
  542.7 2.9 reshape.196
  545.6 2.4 copy.43
  548.1 2.8 copy.52
  551.0 35.4 %reduce-scatter.9.cloned.1.call-done = bf16[384,512]{1,0:T(8,128)(2,1)} async-done(((bf16[1536,512]{1,0:T(8,128)(2,1)}), bf16[384,512]{1,0:T(8,128)(2,1)}) %reduce-scatter.9.cloned.1.call-update) | async-done | bytes 393232
  586.4 1.1 reshape.224
  (56 shorter events, 10.5 us)
Async XLA Ops:
  6.5 332.0 %copy-start = (bf16[1,384,1536]{2,1,0:T(8,128)(2,1)S(1)}, bf16[1,384,1536]{2,1,0:T(8,128)(2,1)}, u32[]{:S(2)}) copy-start(bf16[1,384,1536]{2,1,0:T(8,128)(2,1)} %param.17) | copy-start | bytes 3538948
  6.5 11.7 %copy-start.6 = (f32[8]{0:T(128)S(1)}, f32[8]{0:T(128)}, u32[]{:S(2)}) copy-start(f32[8]{0:T(128)} %param.13) | copy-start | bytes 100
  6.5 92.9 %all-gather.3.cloned.1.call-start = ((), (), s32[]{:S(2)}) async-start(), calls=%async_computation.4 | async-start | bytes 2113536 | tf_op jit(solution)/shard_map/all_gather | solution.py:72
  7.3 117.0 %reduce-scatter.7.cloned.1.call-start = ((), (), s32[]{:S(2)}) async-start(), calls=%async_computation.5 | async-start | bytes 491520
  8.2 8.8 %collective-permute-start = (bf16[128,1,128]{0,2,1:T(8,128)(2,1)S(1)}, bf16[128,1,128]{0,2,1:T(8,128)(2,1)S(1)}, u32[]{:S(2)}, u32[]{:S(2)}) collective-permute-start(bf16[128,1,128]{0,2,1:T(8,128)(2,1)S(1)} %copy.32), channel_id=1, source_target_pairs={{0,4},{4,8},{8,12},{12,16},{16,20},{20,24},{24,28},{28,32},{32,36}... | collective-permute-start | bytes 98312 | tf_op jit(solution)/shard_map/ppermute | solution.py:12
  101.9 1.6 copy-start.3
  101.9 23.3 %copy-start.2 = (bf16[128,384]{1,0:T(8,128)(2,1)S(1)}, bf16[128,384]{1,0:T(8,128)(2,1)}, u32[]{:S(2)}) copy-start(bf16[128,384]{1,0:T(8,128)(2,1)} %param.10) | copy-start | bytes 294916
  101.9 30.3 %copy-start.5 = (f32[384]{0:T(512)S(1)}, f32[384]{0:T(512)}, u32[]{:S(2)}) copy-start(f32[384]{0:T(512)} %param.15) | copy-start | bytes 4612
  355.6 171.5 %all-to-all-start.1 = ((bf16[1,128,12,1536]{3,2,0,1:T(8,128)(2,1)}), bf16[1,128,12,1536]{3,2,0,1:T(8,128)(2,1)}, u32[]{:S(2)}, u32[]{:S(2)}) async-start(bf16[1,128,12,1536]{3,2,0,1:T(8,128)(2,1)} %bitcast.76), calls=%async_computation.1 | async-start | bytes 12582912 | tf_op jit(solution)/shard_map/all_to_all | solution.py:119
  373.2 213.2 %reduce-scatter.9.cloned.1.call-start = ((), (), s32[]{:S(2)}) async-start(), calls=%async_computation.6 | async-start | bytes 1966080
  548.1 2.9 copy-start.4
  550.9 38.5 %copy-start.1 = (bf16[1,384,1536]{2,1,0:T(8,128)(2,1)S(1)}, bf16[1,384,1536]{2,1,0:T(8,128)(2,1)}, u32[]{:S(2)}) copy-start(bf16[1,384,1536]{2,1,0:T(8,128)(2,1)} %param.17) | copy-start | bytes 3538948
Sparse Core Ops, SparseCore 0:
  10.5 88.9 all-gather.2
  103.7 20.4 reduce-scatter.6
  551.1 35.3 reduce-scatter.8
where the time goes:
time: 597 us; the launch traced here: 596 us
  waiting for transfers between devices  293 us (49%)
  blocking collectives  181 us (30%)
  local copies, waits for them, and re-layouts  65.4 us (11%)
  starting transfers between devices  23 us (4%)
  matrix products  17.1 us (3%)
  between operations  13.4 us (2%)
    all_to_all x1, blocking collectives, body(): lax.all_to_all(outbox.reshape(ctx_count, 1, capacity, row_width), 'ctx',...  165 us
    all_to_all x1, waiting for transfers between devices, body(): lax.all_to_all(result, 'ctx', split_axis=1, concat_axis=0, tiled=True)  154 us
    all_gather x1, waiting for transfers between devices, body(): lax.all_gather(out_proj, 'ctx', axis=1, tiled=True)  80.7 us
    unnamed x5, waiting for transfers between devices  56 us
    all_to_all x1, starting transfers between devices, body(): lax.all_to_all(result, 'ctx', split_axis=1, concat_axis=0, tiled=True)  17.5 us
    unnamed x26, local copies, waits for them, and re-layouts  13.2 us
  transfers between devices with their start and end apart: 5, of which 5 were waited for; matrix products, arithmetic and copies ran while one was open for 1% of the time, Pallas kernels for 0%

commit v1 on v0

--- a/solution.py
+++ b/solution.py
@@ -67,10 +67,17 @@
         factor,
     )
     outputs = mixed.reshape(block_row_count, q_heads * head_dim)
+    fix_the_gates = lambda lane_axis, raw, dim_no: jnp.concatenate(
+        lax.all_to_all(
+            jnp.stack([raw for _ in range(lax.axis_size(lane_axis))]),
+            axis_name=lane_axis,
+            split_axis=0,
+            concat_axis=0,
+        ),
+        axis=dim_no,
+    )
     head_partial = jnp.dot(
-        outputs,
-        lax.all_gather(out_proj, "ctx", axis=1, tiled=True),
-        preferred_element_type=jnp.float32,
+        outputs, fix_the_gates("ctx", out_proj, 1), preferred_element_type=jnp.float32
     )
     d_model = head_partial.shape[1]
     residual = hidden_in.astype(jnp.float32) + lax.psum_scatter(

time: 597 us -> 578 us (0.968)
  waiting for transfers between devices: 293 us -> 255 us
  starting transfers between devices: 23 us -> 40.8 us
    all_gather x1 -> x0, waiting for transfers between devices: 80.7 us -> none  [body(): lax.all_gather(out_proj, 'ctx', axis=1, tiled=True)]
    all_to_all x0 -> x1, waiting for transfers between devices: none -> 45.9 us  [body(): lax.all_to_all(jnp.stack([raw for _ in range(lax.axis_size(lane_axis))]),...]
    all_to_all x0 -> x1, starting transfers between devices: none -> 18.5 us  [body(): lax.all_to_all(jnp.stack([raw for _ in range(lax.axis_size(lane_axis))]),...]
    unnamed x26 -> x27, local copies, waits for them, and re-layouts: 13.2 us -> 9.98 us
    unnamed x5 -> x4, waiting for transfers between devices: 56 us -> 54.5 us
where the time goes in v1:
time: 578 us; the launch traced here: 577 us
  waiting for transfers between devices  255 us (44%)
  blocking collectives  181 us (31%)
  local copies, waits for them, and re-layouts  66 us (11%)
  starting transfers between devices  40.8 us (7%)
  matrix products  18.5 us (3%)
  between operations  13.7 us (2%)
    all_to_all x1, blocking collectives, body(): lax.all_to_all(outbox.reshape(ctx_count, 1, capacity, row_width), 'ctx',...  164 us
    all_to_all x1, waiting for transfers between devices, body(): lax.all_to_all(result, 'ctx', split_axis=1, concat_axis=0, tiled=True)  154 us
    unnamed x4, waiting for transfers between devices  54.5 us
    all_to_all x1, waiting for transfers between devices, body(): lax.all_to_all(jnp.stack([raw for _ in range(lax.axis_size(lane_axis))]),...  45.9 us
    all_to_all x1, starting transfers between devices, body(): lax.all_to_all(result, 'ctx', split_axis=1, concat_axis=0, tiled=True)  18.7 us
    all_to_all x1, starting transfers between devices, body(): lax.all_to_all(jnp.stack([raw for _ in range(lax.axis_size(lane_axis))]),...  18.5 us
  transfers between devices with their start and end apart: 5, of which 5 were waited for; matrix products, arithmetic and copies ran while one was open for 1% of the time, Pallas kernels for 0%

profile of v1, /device:TPU:1, one launch (start us, length us, event | category | flops | bytes accessed | tf_op | source)
XLA Modules:
  0.0 576.5 jit_solution(10161527481028939329)
XLA Ops:
  6.5 2.4 stack.2
  9.0 18.5 %all-to-all-start = ((bf16[128,512,12]{1,2,0:T(8,128)(2,1)}), bf16[128,512,12]{1,2,0:T(8,128)(2,1)S(1)}, u32[]{:S(2)}, u32[]{:S(2)}) async-start(bf16[128,512,12]{1,2,0:T(8,128)(2,1)} %stack.2), calls=%async_computation | async-start | bytes 4194304 | tf_op jit(solution)/shard_map/all_to_all | solution.py:71
  27.7 3.5 collective-permute-start
  33.7 45.9 %all-to-all-done = bf16[128,512,12]{1,2,0:T(8,128)(2,1)S(1)} async-done(((bf16[128,512,12]{1,2,0:T(8,128)(2,1)}), bf16[128,512,12]{1,2,0:T(8,128)(2,1)S(1)}, u32[]{:S(2)}, u32[]{:S(2)}) %all-to-all-start) | async-done | bytes 1572896 | tf_op jit(solution)/shard_map/all_to_all | solution.py:71
  81.0 2.1 convolution_convert_fusion.1
  84.9 19.0 %reduce-scatter.7.cloned.1.call-done = bf16[384,128]{1,0:T(8,128)(2,1)} async-done(((bf16[1536,128]{1,0:T(8,128)(2,1)}), bf16[384,128]{1,0:T(8,128)(2,1)}) %reduce-scatter.7.cloned.1.call-update) | async-done | bytes 98320
  105.0 6.8 %psum.7 = f32[128]{0:T(128)S(1)} all-reduce(f32[128]{0:T(128)S(1)} %multiply_reduce_fusion), channel_id=1, replica_groups=mesh['ctx'=128,'tp'=4] {'tp'}, use_global_device_ids=true, to_apply=%region_8.9 | all-reduce | flops 128 | bytes 1024 | tf_op jit(solution)/shard_map/psum | solution.py:86
  111.9 10.0 %all_gather.3 = bf16[128,1536]{1,0:T(8,128)(2,1)S(1)} all-gather(bf16[128,384]{1,0:T(8,128)(2,1)S(1)} %multiply_convert_fusion), channel_id=1, replica_groups=mesh['ctx'=128,'tp'=4] {'tp'}, dimensions={1}, use_global_device_ids=true | all-gather | bytes 491520 | tf_op jit(solution)/shard_map/all_gather | solution.py:102
  122.4 1.4 reshape.223
  123.8 6.9 %scatter_custom_fusion = bf16[1536,1536]{1,0:T(8,128)(2,1)} fusion(s32[512]{0:T(512)S(1)} %bitcast.86, bf16[512,1536]{1,0:T(8,128)(2,1)} %reshape.223, bf16[]{:T(256)} %constant.14.clone.1), kind=kCustom, calls=%fused_computation.8 | custom fusion | bytes 4719104 | tf_op jit(solution)/shard_map/scatter | solution.py:107
  130.6 8.1 %reshape.202 = bf16[128,1,12,1536]{3,2,0,1:T(8,128)(2,1)} reshape(bf16[1536,1536]{1,0:T(8,128)(2,1)} %scatter_custom_fusion) | data formatting | bytes 9437184 | tf_op jit(solution)/shard_map/reshape | solution.py:109
  138.7 164.0 %all_to_all.23 = bf16[128,1,12,1536]{3,2,1,0:T(8,128)(2,1)} all-to-all(bf16[128,1,12,1536]{3,2,1,0:T(8,128)(2,1)} %bitcast.77), channel_id=1, replica_groups=mesh['ctx'=128,'tp'=4] {'ctx'}, dimensions={0} | all-to-all | bytes 9437184 | tf_op jit(solution)/shard_map/all_to_all | solution.py:108
  302.7 8.2 %reshape.203 = bf16[1536,1536]{1,0:T(8,128)(2,1)} reshape(bf16[128,1,12,1536]{3,2,1,0:T(8,128)(2,1)} %all_to_all.23) | data formatting | bytes 9437184 | tf_op jit(solution)/shard_map/reshape | solution.py:116
  310.9 6.7 %fusion.7 = f32[1536,384]{1,0:T(8,128)} fusion(bf16[1536,1536]{1,0:T(8,128)(2,1)} %reshape.203, bf16[1,2,1536,384]{3,2,1,0:T(8,128)(2,1)} %param.16), kind=kOutput, calls=%fused_computation.14 | convolution fusion | flops 1811939328 | bytes 8257536 | tf_op jit(solution)/shard_map/dot_general | solution.py:117
  317.6 9.1 %convolution_convert_fusion = bf16[1536,1536]{1,0:T(8,128)(2,1)} fusion(bf16[1,384,1536]{2,1,0:T(8,128)(2,1)S(1)} %copy-done, f32[1536,384]{1,0:T(8,128)} %fusion.7, bf16[1536,1536]{1,0:T(8,128)(2,1)} %reshape.203, bf16[1,2,1536,384]{3,2,1,0:T(8,128)(2,1)} %param.16), kind=kOutput, calls=%fused_computation.2 | convolution fusion | flops 3630956544 | bytes 14155776 | tf_op jit(solution)/shard_map/dot_general | solution.py:122
  326.6 8.1 %reshape.204 = bf16[1,128,12,1536]{3,2,1,0:T(8,128)(2,1)} reshape(bf16[1536,1536]{1,0:T(8,128)(2,1)} %convolution_convert_fusion) | data formatting | bytes 9437184 | tf_op jit(solution)/shard_map/reshape | solution.py:125
  334.7 18.7 %all-to-all-start.2 = ((bf16[1,128,12,1536]{3,2,0,1:T(8,128)(2,1)}), bf16[1,128,12,1536]{3,2,0,1:T(8,128)(2,1)}, u32[]{:S(2)}, u32[]{:S(2)}) async-start(bf16[1,128,12,1536]{3,2,0,1:T(8,128)(2,1)} %bitcast.76), calls=%async_computation.2 | async-start | bytes 12582912 | tf_op jit(solution)/shard_map/all_to_all | solution.py:126
  353.4 153.9 %all-to-all-done.2 = bf16[1,128,12,1536]{3,2,0,1:T(8,128)(2,1)} async-done(((bf16[1,128,12,1536]{3,2,0,1:T(8,128)(2,1)}), bf16[1,128,12,1536]{3,2,0,1:T(8,128)(2,1)}, u32[]{:S(2)}, u32[]{:S(2)}) %all-to-all-start.2) | async-done | bytes 4718624 | tf_op jit(solution)/shard_map/all_to_all | solution.py:126
  507.3 8.2 %reshape.205 = bf16[1536,1536]{1,0:T(8,128)(2,1)} reshape(bf16[1,128,12,1536]{3,2,0,1:T(8,128)(2,1)} %all-to-all-done.2) | data formatting | bytes 9437184 | tf_op jit(solution)/shard_map/reshape | solution.py:127
  515.6 7.4 %gather_fusion = bf16[512,1536]{1,0:T(8,128)(2,1)} fusion(bf16[1536,1536]{1,0:T(8,128)(2,1)} %reshape.205, s32[1024]{0:T(1024)S(1)} %pad_clamp_fusion), kind=kCustom, calls=%fused_computation | custom fusion | bytes 3147776 | tf_op jit(solution)/shard_map/gather | solution.py:127
  522.9 2.9 reshape.206
  525.8 2.4 copy.44
  528.2 2.8 copy.53
  531.2 35.5 %reduce-scatter.9.cloned.1.call-done = bf16[384,512]{1,0:T(8,128)(2,1)} async-done(((bf16[1536,512]{1,0:T(8,128)(2,1)}), bf16[384,512]{1,0:T(8,128)(2,1)}) %reduce-scatter.9.cloned.1.call-update) | async-done | bytes 393232
  (58 shorter events, 10.4 us)
Async XLA Ops:
  6.5 311.1 %copy-start = (bf16[1,384,1536]{2,1,0:T(8,128)(2,1)S(1)}, bf16[1,384,1536]{2,1,0:T(8,128)(2,1)}, u32[]{:S(2)}) copy-start(bf16[1,384,1536]{2,1,0:T(8,128)(2,1)} %param.17) | copy-start | bytes 3538948
  9.0 18.6 %copy-start.3 = (bf16[128,1,128]{2,0,1:T(8,128)(2,1)S(1)}, bf16[128,1,128]{2,0,1:T(8,128)(2,1)}, u32[]{:S(2)}) copy-start(bf16[128,1,128]{2,0,1:T(8,128)(2,1)} %param.12) | copy-start | bytes 98308
  9.0 24.0 %copy-start.7 = (f32[8]{0:T(128)S(1)}, f32[8]{0:T(128)}, u32[]{:S(2)}) copy-start(f32[8]{0:T(128)} %param.13) | copy-start | bytes 100
  9.0 70.7 %all-to-all-start = ((bf16[128,512,12]{1,2,0:T(8,128)(2,1)}), bf16[128,512,12]{1,2,0:T(8,128)(2,1)S(1)}, u32[]{:S(2)}, u32[]{:S(2)}) async-start(bf16[128,512,12]{1,2,0:T(8,128)(2,1)} %stack.2), calls=%async_computation | async-start | bytes 4194304 | tf_op jit(solution)/shard_map/all_to_all | solution.py:71
  27.5 76.3 %reduce-scatter.7.cloned.1.call-start = ((), (), s32[]{:S(2)}) async-start(), calls=%async_computation.5 | async-start | bytes 491520
  27.7 5.0 collective-permute-start
  81.0 3.0 copy-start.4
  81.0 23.9 %copy-start.2 = (bf16[128,384]{1,0:T(8,128)(2,1)S(1)}, bf16[128,384]{1,0:T(8,128)(2,1)}, u32[]{:S(2)}) copy-start(bf16[128,384]{1,0:T(8,128)(2,1)} %param.10) | copy-start | bytes 294916
  81.0 30.9 %copy-start.6 = (f32[384]{0:T(512)S(1)}, f32[384]{0:T(512)}, u32[]{:S(2)}) copy-start(f32[384]{0:T(512)} %param.15) | copy-start | bytes 4612
  334.7 172.6 %all-to-all-start.2 = ((bf16[1,128,12,1536]{3,2,0,1:T(8,128)(2,1)}), bf16[1,128,12,1536]{3,2,0,1:T(8,128)(2,1)}, u32[]{:S(2)}, u32[]{:S(2)}) async-start(bf16[1,128,12,1536]{3,2,0,1:T(8,128)(2,1)} %bitcast.76), calls=%async_computation.2 | async-start | bytes 12582912 | tf_op jit(solution)/shard_map/all_to_all | solution.py:126
  353.4 213.3 %reduce-scatter.9.cloned.1.call-start = ((), (), s32[]{:S(2)}) async-start(), calls=%async_computation.6 | async-start | bytes 1966080
  528.2 2.9 copy-start.5
  531.1 38.6 %copy-start.1 = (bf16[1,384,1536]{2,1,0:T(8,128)(2,1)S(1)}, bf16[1,384,1536]{2,1,0:T(8,128)(2,1)}, u32[]{:S(2)}) copy-start(bf16[1,384,1536]{2,1,0:T(8,128)(2,1)} %param.17) | copy-start | bytes 3538948
Sparse Core Ops, SparseCore 0:
  84.1 19.6 reduce-scatter.6
  531.2 35.3 reduce-scatter.8
